TPU v7x, 512 devices: a whole 4x8x8 slice. The times are simulated.
512 devices in a mesh: lat: 64 (over y, x, core), row: 8 (over z).
Axes of the slice: x: 4, y: 8, z: 8, core: 2. Of those that a mesh axis runs over, the one named last changes fastest.
Arguments:
- activations: float32 [12288, 8192], P('lat', 'row'), may hold values from -15 to 15
- center_bias: float32 [8192], P('row'), may hold values from -3 to 3
- encoder_weight: bfloat16 [8192, 16384], P('row', 'lat'), may hold values from -0.0625 to 0.0625
- encoder_bias: float32 [16384], P('lat'), may hold values from -3 to 3
- decoder_weight: bfloat16 [16384, 8192], P('lat', 'row'), may hold values from -1 to 1
- row_blocks: int32 [12288, 4], P('lat'), may hold values from 0 to 127, all different within a row; in each aligned block of 192 rows (0 to 191, 192 to 383, ...) at most 12 rows name the same one
- pick_offsets: int32 [12288, 4, 8], P('lat'), may hold values from 0 to 127
Outputs:
- encoder_grad: bfloat16 [8192, 16384], P('row', 'lat')
- decoder_grad: bfloat16 [16384, 8192], P('lat', 'row')
- bias_grad: float32 [16384], P('lat')
- row_loss: float32 [12288], P('lat')
Inputs may be any that keep to these rules, and one draw needn't show every extreme that they name: `row_blocks`: the 4 blocks of a row differ. Within each group of 192 rows (the rows of one lat index), at most 12 rows name the same block, and in some groups one block is named by exactly 12 rows.
All inputs are finite; a program needn't handle non-finite values.
Results may differ from a plain program's by a relative error of at most 0.006.
Values may be sent and summed in bfloat16 or wider, within the bound.
No kernel may reach another device: no remote copies, remote signals or barrier semaphores. Data moves between devices by JAX's collectives and lax.ppermute only.
A program may use at most 64 MiB of HBM per device.

v0:
```python
import jax
import jax.numpy as jnp
from jax import lax
from jax.sharding import PartitionSpec as P

D = 8192
BLK = 128
KB = 4
PER = 8


def slot_targets(row_blocks, total_blocks, capacity):
    pair_blocks = row_blocks.reshape(-1)
    onehot = (pair_blocks[:, None] == jnp.arange(total_blocks, dtype=jnp.int32)[None, :]).astype(
        jnp.int32
    )
    before = jnp.cumsum(onehot, axis=0) - onehot
    ranking = jnp.sum(before * onehot, axis=1)
    return pair_blocks * capacity + ranking


def pick_columns(values, offsets):
    lanes = jnp.arange(BLK, dtype=jnp.int32)
    hit = offsets[:, :, None] == lanes[None, None, :]
    return jnp.sum(jnp.where(hit, values[:, None, :], 0.0), axis=2)


def spread_columns(picked, offsets):
    lanes = jnp.arange(BLK, dtype=jnp.int32)[None, :]
    out = jnp.zeros((picked.shape[0], BLK), picked.dtype)
    for j in range(PER):
        out = jnp.where(offsets[:, j : j + 1] == lanes, picked[:, j : j + 1], out)
    return out


def per_device(
    activations, center_bias, encoder_weight, encoder_bias, decoder_weight, row_blocks, pick_offsets
):
    group_rows, feature_width = activations.shape
    owners = lax.axis_size("lat")
    owned_blocks = encoder_bias.shape[0] // BLK
    total_blocks = owned_blocks * owners
    capacity = 2 * group_rows * KB // total_blocks
    slot_count = total_blocks * capacity
    per_owner = owned_blocks * capacity
    target = slot_targets(row_blocks, total_blocks, capacity)
    slots = jnp.arange(slot_count, dtype=jnp.int32)
    pair_hot = target[None, :] == slots[:, None]
    row_hot = jnp.any(pair_hot.reshape(slot_count, group_rows, KB), axis=2).astype(jnp.bfloat16)
    pair_hot = pair_hot.astype(jnp.bfloat16)
    centered = (activations - center_bias[None, :]).astype(jnp.bfloat16)
    outgoing = jnp.dot(row_hot, centered, preferred_element_type=jnp.float32).astype(jnp.bfloat16)
    offs_plus = (pick_offsets.reshape(-1, PER) + 1).astype(jnp.bfloat16)
    out_offs = jnp.dot(pair_hot, offs_plus, preferred_element_type=jnp.float32).astype(jnp.int32)
    got_offs = lax.all_to_all(
        out_offs.reshape(owners, per_owner, PER), "lat", split_axis=0, concat_axis=0, tiled=True
    )
    got_rows = lax.all_to_all(
        outgoing.reshape(owners, per_owner, feature_width),
        "lat",
        split_axis=0,
        concat_axis=0,
        tiled=True,
    )
    got_rows = got_rows.reshape(slot_count, feature_width)
    offs = got_offs.reshape(slot_count, PER) - 1
    slot_block = slots // capacity % owned_blocks
    col_block = jnp.arange(owned_blocks * BLK, dtype=jnp.int32) // BLK
    own_col = slot_block[:, None] == col_block[None, :]

    def own_half(full):
        parts = full.reshape(slot_count, owned_blocks, BLK)
        sel = slot_block[:, None, None] == jnp.arange(owned_blocks, dtype=jnp.int32)[None, :, None]
        return jnp.sum(jnp.where(sel, parts, 0.0), axis=1)

    def widen(narrow):
        tiled = jnp.tile(narrow, (1, owned_blocks))
        return jnp.where(own_col, tiled, jnp.zeros_like(tiled))

    partial_full = jnp.dot(got_rows, encoder_weight, preferred_element_type=jnp.float32)
    partial = pick_columns(own_half(partial_full), offs)
    summed = lax.psum(partial, "row")
    bias_rows = own_half(jnp.broadcast_to(encoder_bias[None, :], (slot_count, owned_blocks * BLK)))
    pre_picked = summed + pick_columns(bias_rows, offs)
    latent = spread_columns(pre_picked, offs).astype(jnp.bfloat16)
    latent_wide = widen(latent)
    decoded = jnp.dot(latent_wide, decoder_weight, preferred_element_type=jnp.float32).astype(
        jnp.bfloat16
    )
    returned = lax.all_to_all(
        decoded.reshape(owners, per_owner, feature_width),
        "lat",
        split_axis=0,
        concat_axis=0,
        tiled=True,
    ).reshape(slot_count, feature_width)
    rebuilt = lax.dot_general(
        row_hot, returned, (((0,), (0,)), ((), ())), preferred_element_type=jnp.float32
    )
    recon_error = center_bias[None, :] + rebuilt - activations
    loss_part = jnp.sum(recon_error * recon_error, axis=1)
    error_b = recon_error.astype(jnp.bfloat16)
    out_error = jnp.dot(row_hot, error_b, preferred_element_type=jnp.float32).astype(jnp.bfloat16)
    got_error = lax.all_to_all(
        out_error.reshape(owners, per_owner, feature_width),
        "lat",
        split_axis=0,
        concat_axis=0,
        tiled=True,
    ).reshape(slot_count, feature_width)
    decoder_grad = lax.dot_general(
        latent_wide, got_error, (((0,), (0,)), ((), ())), preferred_element_type=jnp.float32
    ).astype(jnp.bfloat16)
    dlatent_full = lax.dot_general(
        got_error, decoder_weight, (((1,), (1,)), ((), ())), preferred_element_type=jnp.float32
    )
    dlatent_part = pick_columns(own_half(dlatent_full), offs)
    dlatent, loss_total = lax.psum((dlatent_part, loss_part), "row")
    grad_pre = spread_columns(dlatent, offs).astype(jnp.bfloat16)
    grad_wide = widen(grad_pre)
    encoder_grad = lax.dot_general(
        got_rows, grad_wide, (((0,), (0,)), ((), ())), preferred_element_type=jnp.float32
    ).astype(jnp.bfloat16)
    bias_grad = jnp.sum(grad_wide.astype(jnp.float32), axis=0)
    row_loss = loss_total / D
    return (encoder_grad, decoder_grad, bias_grad, row_loss)


def solution(mesh):
    return jax.shard_map(
        per_device,
        mesh=mesh,
        in_specs=(
            P("lat", "row"),
            P("row"),
            P("row", "lat"),
            P("lat"),
            P("lat", "row"),
            P("lat", None),
            P("lat", None, None),
        ),
        out_specs=(P("row", "lat"), P("lat", "row"), P("lat"), P("lat")),
        check_vma=False,
    )
```

profile of v0, /device:TPU:4, one launch (start us, length us, event | category | flops | bytes accessed | tf_op | source)
XLA Modules:
  0.0 398.2 jit_solution(482381687215918004)
XLA Ops:
  0.7 0.9 copy.46
  2.8 0.9 fusion.3
  4.0 0.9 reshape.842
  4.9 10.6 %all-to-all-start.1 = ((s32[64,1,192]{2,1,0:T(1,128)}), s32[64,1,192]{2,1,0:T(1,128)S(1)}, u32[]{:S(2)}, u32[]{:S(2)}) async-start(s32[64,1,192]{2,1,0:T(1,128)} %reshape.842), calls=%async_computation.1 | async-start | bytes 131072 | tf_op jit(solution)/shard_map/all_to_all | solution.py:55
  15.7 1.0 fusion
  16.8 2.8 convolution_convert_fusion.2
  19.6 4.1 %all-to-all-done.1 = s32[64,1,192]{2,1,0:T(1,128)S(1)} async-done(((s32[64,1,192]{2,1,0:T(1,128)}), s32[64,1,192]{2,1,0:T(1,128)S(1)}, u32[]{:S(2)}, u32[]{:S(2)}) %all-to-all-start.1) | async-done | bytes 49184 | tf_op jit(solution)/shard_map/all_to_all | solution.py:55
  23.7 7.4 %all-to-all-start = ((bf16[64,24,1024]{2,1,0:T(8,128)(2,1)}), bf16[64,24,1024]{2,1,0:T(8,128)(2,1)}, u32[]{:S(2)}, u32[]{:S(2)}) async-start(bf16[64,24,1024]{2,1,0:T(8,128)(2,1)} %bitcast.63), calls=%async_computation | async-start | bytes 6291456 | tf_op jit(solution)/shard_map/all_to_all | solution.py:58
  31.4 0.6 select_reduce_fusion.3
  32.5 0.8 reduce.49
  34.4 70.5 %all-to-all-done = bf16[64,24,1024]{2,1,0:T(8,128)(2,1)} async-done(((bf16[64,24,1024]{2,1,0:T(8,128)(2,1)}), bf16[64,24,1024]{2,1,0:T(8,128)(2,1)}, u32[]{:S(2)}, u32[]{:S(2)}) %all-to-all-start) | async-done | bytes 3145760 | tf_op jit(solution)/shard_map/all_to_all | solution.py:58
  104.9 4.0 %fusion.4 = f32[1536,128]{1,0:T(8,128)S(1)} fusion(bf16[1536,1024,1]{1,0,2:T(8,128)(2,1)} %bitcast.6, bf16[2,128,1024]{2,1,0:T(8,128)(2,1)S(1)} %bitcast.73, pred[1536,2]{0,1:T(4,128)(4,1)S(1)} %iota_compare_fusion.17), kind=kOutput, calls=%fused_computation.21 | convolution fusion | flops 805896192 | bytes 4459520 | tf_op jit(solution)/shard_map/dot_general | solution.py:80
  108.9 8.5 %select_reduce_fusion.1 = (f32[1536,8]{1,0:T(8,128)}, f32[1536,8]{1,0:T(8,128)S(1)}) fusion(f32[1536,128]{1,0:T(8,128)S(1)} %select_reduce_fusion.3, s32[1536,8]{1,0:T(8,128)S(1)} %copy.55, f32[1536,128]{1,0:T(8,128)S(1)} %fusion.4), kind=kLoop, calls=%fused_computation.1 | loop fusion | flops 7839744 | bytes 1720320 | tf_op jit(solution)/shard_map/reduce_sum | solution.py:25
  117.3 42.3 %psum.21 = f32[1536,8]{1,0:T(8,128)S(1)} all-reduce(f32[1536,8]{1,0:T(8,128)S(1)} %get-tuple-element.21), channel_id=1, replica_groups=mesh['lat'=64,'row'=8] {'row'}, use_global_device_ids=true, to_apply=%region_6.7 | all-reduce | flops 12288 | bytes 98304 | tf_op jit(solution)/shard_map/psum | solution.py:82
  159.6 1.2 add.87
  160.8 3.1 slice_reduce_fusion.15
  163.9 3.8 select_convert_fusion.1
  168.2 1.0 convolution_convert_fusion.1
  169.2 80.9 %all_to_all.20 = bf16[64,24,1024]{2,1,0:T(8,128)(2,1)S(1)} all-to-all(bf16[64,24,1024]{2,1,0:T(8,128)(2,1)S(1)} %bitcast.66), channel_id=1, replica_groups=mesh['lat'=64,'row'=8] {'lat'}, dimensions={0} | all-to-all | bytes 6291456 | tf_op jit(solution)/shard_map/all_to_all | solution.py:90
  250.1 0.9 multiply_reduce_fusion
  251.1 2.8 convolution_convert_fusion
  253.9 5.8 %all-to-all-start.3 = ((bf16[64,24,1024]{2,1,0:T(8,128)(2,1)}), bf16[64,24,1024]{2,1,0:T(8,128)(2,1)}, u32[]{:S(2)}, u32[]{:S(2)}) async-start(bf16[64,24,1024]{2,1,0:T(8,128)(2,1)} %bitcast.64), calls=%async_computation.3 | async-start | bytes 6291456 | tf_op jit(solution)/shard_map/all_to_all | solution.py:104
  259.7 73.6 %all-to-all-done.3 = bf16[64,24,1024]{2,1,0:T(8,128)(2,1)} async-done(((bf16[64,24,1024]{2,1,0:T(8,128)(2,1)}), bf16[64,24,1024]{2,1,0:T(8,128)(2,1)}, u32[]{:S(2)}, u32[]{:S(2)}) %all-to-all-start.3) | async-done | bytes 3145760 | tf_op jit(solution)/shard_map/all_to_all | solution.py:104
  333.4 4.0 fusion.5
  337.4 4.8 %select_reduce_fusion = f32[1536,8]{1,0:T(8,128)S(1)} fusion(f32[1536,128]{1,0:T(8,128)S(1)} %fusion.5, s32[1536,8]{1,0:T(8,128)S(1)} %copy.55), kind=kLoop, calls=%fused_computation | loop fusion | flops 4706304 | bytes 884736 | tf_op jit(solution)/shard_map/reduce_sum | solution.py:25
  342.2 35.4 %all-reduce = (f32[1536,8]{1,0:T(8,128)S(1)}, f32[192]{0:T(256)S(1)}) all-reduce(f32[1536,8]{1,0:T(8,128)S(1)} %select_reduce_fusion, f32[192]{0:T(256)S(1)} %get-tuple-element.34), channel_id=1, replica_groups=mesh['lat'=64,'row'=8] {'row'}, use_global_device_ids=true, to_apply=%region_11.12 | all-reduce | flops 12480 | bytes 99840 | tf_op jit(solution)/shard_map/psum | solution.py:118
  377.6 3.1 slice_reduce_fusion.7
  380.8 3.8 select_convert_fusion
  384.6 4.8 %compare_select_fusion = (bf16[1536,2,128]{2,1,0:T(2,128)(2,1)S(1)}, bf16[1536,2,128]{2,1,0:T(2,128)(2,1)S(1)}) fusion(s32[2,128]{1,0:T(2,128)S(1)} %and_select_fusion.1, s32[1536]{0:T(1024)S(1)} %add_select_fusion, bf16[1536,128]{1,0:T(8,128)(2,1)S(1)} %select_convert_fusion.1, bf16[1536,128]{1,0:T(8,128)(2,1)S(1)} %select_convert_fusion), kind=kLoop, calls=%fused_computation.11 | loop fusion | flops 1179648 | bytes 2366464 | tf_op jit(solution)/shard_map/jit(_where)/select_n | solution.py:78
  389.3 0.8 convert_reduce_fusion
  390.7 3.7 convolution_convert_fusion.3
  394.4 3.7 convolution_convert_fusion.4
  (48 shorter events, 4.5 us)
Async XLA Ops:
  0.6 167.6 %copy-start = (bf16[256,1024]{1,0:T(8,128)(2,1)S(1)}, bf16[256,1024]{1,0:T(8,128)(2,1)}, u32[]{:S(2)}) copy-start(bf16[256,1024]{1,0:T(8,128)(2,1)} %param.11) | copy-start | bytes 1572868
  0.6 1.9 copy-start.4
  1.5 14.2 %copy-start.5 = (s32[192,4]{0,1:T(4,128)S(1)}, s32[192,4]{0,1:T(4,128)}, u32[]{:S(2)}) copy-start(s32[192,4]{0,1:T(4,128)} %param.12) | copy-start | bytes 9220
  1.9 14.9 %copy-start.1 = (f32[192,1024]{1,0:T(8,128)S(1)}, f32[192,1024]{1,0:T(8,128)}, u32[]{:S(2)}) copy-start(f32[192,1024]{1,0:T(8,128)} %param.7) | copy-start | bytes 2359300
  1.9 14.9 %copy-start.6 = (f32[1024]{0:T(1024)S(1)}, f32[1024]{0:T(1024)}, u32[]{:S(2)}) copy-start(f32[1024]{0:T(1024)} %param.8) | copy-start | bytes 12292
  4.9 18.8 %all-to-all-start.1 = ((s32[64,1,192]{2,1,0:T(1,128)}), s32[64,1,192]{2,1,0:T(1,128)S(1)}, u32[]{:S(2)}, u32[]{:S(2)}) async-start(s32[64,1,192]{2,1,0:T(1,128)} %reshape.842), calls=%async_computation.1 | async-start | bytes 131072 | tf_op jit(solution)/shard_map/all_to_all | solution.py:55
  23.7 7.4 %copy-start.3 = (bf16[1024,256]{1,0:T(8,128)(2,1)S(1)}, bf16[1024,256]{1,0:T(8,128)(2,1)}, u32[]{:S(2)}) copy-start(bf16[1024,256]{1,0:T(8,128)(2,1)} %param.9) | copy-start | bytes 1572868
  23.7 7.7 %copy-start.7 = (f32[256]{0:T(256)S(1)}, f32[256]{0:T(256)}, u32[]{:S(2)}) copy-start(f32[256]{0:T(256)} %param.10) | copy-start | bytes 3076
  23.7 81.2 %all-to-all-start = ((bf16[64,24,1024]{2,1,0:T(8,128)(2,1)}), bf16[64,24,1024]{2,1,0:T(8,128)(2,1)}, u32[]{:S(2)}, u32[]{:S(2)}) async-start(bf16[64,24,1024]{2,1,0:T(8,128)(2,1)} %bitcast.63), calls=%async_computation | async-start | bytes 6291456 | tf_op jit(solution)/shard_map/all_to_all | solution.py:58
  169.2 80.9 %copy-start.2 = (f32[192,1024]{1,0:T(8,128)S(1)}, f32[192,1024]{1,0:T(8,128)}, u32[]{:S(2)}) copy-start(f32[192,1024]{1,0:T(8,128)} %param.7) | copy-start | bytes 2359300
  253.9 79.5 %all-to-all-start.3 = ((bf16[64,24,1024]{2,1,0:T(8,128)(2,1)}), bf16[64,24,1024]{2,1,0:T(8,128)(2,1)}, u32[]{:S(2)}, u32[]{:S(2)}) async-start(bf16[64,24,1024]{2,1,0:T(8,128)(2,1)} %bitcast.64), calls=%async_computation.3 | async-start | bytes 6291456 | tf_op jit(solution)/shard_map/all_to_all | solution.py:104
where the time goes:
time: 399 us; the launch traced here: 398 us
  blocking collectives  159 us (40%)
  waiting for transfers between devices  148 us (37%)
  other arithmetic  31.3 us (8%)
  matrix products  23.9 us (6%)
  starting transfers between devices  23.8 us (6%)
  local copies, waits for them, and re-layouts  11.3 us (3%)
    all_to_all x1, blocking collectives, per_device(): lax.all_to_all(decoded.reshape(owners, per_owner, feature_width), 'lat',...  80.9 us
    all_to_all x1, waiting for transfers between devices, per_device(): lax.all_to_all(out_error.reshape(owners, per_owner, feature_width), 'lat'...  73.6 us
    all_to_all x1, waiting for transfers between devices, per_device(): lax.all_to_all(outgoing.reshape(owners, per_owner, feature_width), 'lat',...  70.5 us
    psum x1, blocking collectives, per_device(): summed = lax.psum(partial, 'row')  42.3 us
    psum x1, blocking collectives, per_device(): dlatent, loss_total = lax.psum((dlatent_part, loss_part), 'row')  35.4 us
    reduce_sum x2, other arithmetic, pick_columns(): return jnp.sum(jnp.where(hit, values[:, None, :], 0.0), axis=2)  13.3 us
    all_to_all x1, starting transfers between devices, per_device(): lax.all_to_all(out_offs.reshape(owners, per_owner, PER), 'lat', split_axi...  10.6 us
  transfers between devices with their start and end apart: 3, of which 3 were waited for; matrix products, arithmetic and copies ran while one was open for 2% of the time, Pallas kernels for 0%

commit v1 on v0

--- a/solution.py
+++ b/solution.py
@@ -79,7 +79,7 @@
 
     partial_full = jnp.dot(got_rows, encoder_weight, preferred_element_type=jnp.float32)
     partial = pick_columns(own_half(partial_full), offs)
-    summed = lax.psum(partial, "row")
+    summed = jnp.sum(lax.all_gather(partial, "row"), axis=0)
     bias_rows = own_half(jnp.broadcast_to(encoder_bias[None, :], (slot_count, owned_blocks * BLK)))
     pre_picked = summed + pick_columns(bias_rows, offs)
     latent = spread_columns(pre_picked, offs).astype(jnp.bfloat16)

time: 399 us -> 427 us (1.070)
  the two profiles are of different devices: /device:TPU:4 before, /device:TPU:8 now
where the time goes in v1:
time: 427 us
  blocking collectives  187 us (44%)
  waiting for transfers between devices  147 us (34%)
  other arithmetic  34.1 us (8%)
  matrix products  23.9 us (6%)
  starting transfers between devices  23.8 us (6%)
  local copies, waits for them, and re-layouts  9.84 us (2%)
    all_to_all x1, blocking collectives, per_device(): lax.all_to_all(decoded.reshape(owners, per_owner, feature_width), 'lat',...  79.1 us
    all_to_all x1, waiting for transfers between devices, per_device(): lax.all_to_all(out_error.reshape(owners, per_owner, feature_width), 'lat'...  72.8 us
    all_gather x1, blocking collectives, per_device(): summed = jnp.sum(lax.all_gather(partial, 'row'), axis=0)  69.9 us
    all_to_all x1, waiting for transfers between devices, per_device(): lax.all_to_all(outgoing.reshape(owners, per_owner, feature_width), 'lat',...  69.6 us
    psum x1, blocking collectives, per_device(): dlatent, loss_total = lax.psum((dlatent_part, loss_part), 'row')  37.6 us
    reduce_sum x2, other arithmetic, pick_columns(): return jnp.sum(jnp.where(hit, values[:, None, :], 0.0), axis=2)  13.3 us
    all_to_all x1, starting transfers between devices, per_device(): lax.all_to_all(out_offs.reshape(owners, per_owner, PER), 'lat', split_axi...  10.6 us
  transfers between devices with their start and end apart: 3, of which 3 were waited for; matrix products, arithmetic and copies ran while one was open for 2% of the time, Pallas kernels for 0%

profile of v1, /device:TPU:8, one launch (start us, length us, event | category | flops | bytes accessed | tf_op | source)
XLA Modules:
  0.0 426.6 jit_solution(4217086036829463737)
XLA Ops:
  0.6 0.9 copy.48
  1.7 0.8 add_convert_fusion
  3.5 0.9 fusion.3
  4.8 0.9 reshape.843
  5.6 10.6 %all-to-all-start.1 = ((s32[64,1,192]{2,1,0:T(1,128)}), s32[64,1,192]{2,1,0:T(1,128)S(1)}, u32[]{:S(2)}, u32[]{:S(2)}) async-start(s32[64,1,192]{2,1,0:T(1,128)} %reshape.843), calls=%async_computation.1 | async-start | bytes 131072 | tf_op jit(solution)/shard_map/all_to_all | solution.py:55
  16.4 1.0 fusion
  17.4 2.8 convolution_convert_fusion.2
  20.2 5.1 %all-to-all-done.1 = s32[64,1,192]{2,1,0:T(1,128)S(1)} async-done(((s32[64,1,192]{2,1,0:T(1,128)}), s32[64,1,192]{2,1,0:T(1,128)S(1)}, u32[]{:S(2)}, u32[]{:S(2)}) %all-to-all-start.1) | async-done | bytes 49184 | tf_op jit(solution)/shard_map/all_to_all | solution.py:55
  25.3 6.5 %all-to-all-start = ((bf16[64,24,1024]{2,1,0:T(8,128)(2,1)}), bf16[64,24,1024]{2,1,0:T(8,128)(2,1)}, u32[]{:S(2)}, u32[]{:S(2)}) async-start(bf16[64,24,1024]{2,1,0:T(8,128)(2,1)} %bitcast.65), calls=%async_computation | async-start | bytes 6291456 | tf_op jit(solution)/shard_map/all_to_all | solution.py:58
  33.2 0.8 reduce.49
  35.1 69.6 %all-to-all-done = bf16[64,24,1024]{2,1,0:T(8,128)(2,1)} async-done(((bf16[64,24,1024]{2,1,0:T(8,128)(2,1)}), bf16[64,24,1024]{2,1,0:T(8,128)(2,1)}, u32[]{:S(2)}, u32[]{:S(2)}) %all-to-all-start) | async-done | bytes 3145760 | tf_op jit(solution)/shard_map/all_to_all | solution.py:58
  104.7 4.0 fusion.4
  108.7 8.4 %select_reduce_fusion.1 = (f32[1536,8]{1,0:T(8,128)}, f32[1536,8]{1,0:T(8,128)S(1)}) fusion(f32[1536,128]{1,0:T(8,128)S(1)} %select_reduce_fusion.3, s32[1536,8]{1,0:T(8,128)S(1)} %copy.57, f32[1536,128]{1,0:T(8,128)S(1)} %fusion.4), kind=kLoop, calls=%fused_computation.1 | loop fusion | flops 7839744 | bytes 1720320 | tf_op jit(solution)/shard_map/reduce_sum | solution.py:25
  117.1 1.4 copy.60
  118.5 69.9 %all-gather = f32[12288,8]{1,0:T(8,128)} all-gather(f32[1536,8]{1,0:T(8,128)S(1)} %get-tuple-element.13), channel_id=2, replica_groups=mesh['lat'=64,'row'=8] {'row'}, dimensions={0}, use_global_device_ids=true | all-gather | bytes 442368 | tf_op jit(solution)/shard_map/all_gather | solution.py:82
  188.4 3.3 reduce_sum.98
  192.1 3.8 select_convert_fusion.1
  196.3 1.0 convolution_convert_fusion.1
  197.4 79.1 %all_to_all.20 = bf16[64,24,1024]{2,1,0:T(8,128)(2,1)S(1)} all-to-all(bf16[64,24,1024]{2,1,0:T(8,128)(2,1)S(1)} %bitcast.68), channel_id=1, replica_groups=mesh['lat'=64,'row'=8] {'lat'}, dimensions={0} | all-to-all | bytes 6291456 | tf_op jit(solution)/shard_map/all_to_all | solution.py:90
  276.5 0.9 multiply_reduce_fusion
  277.4 2.8 convolution_convert_fusion
  280.2 6.7 %all-to-all-start.3 = ((bf16[64,24,1024]{2,1,0:T(8,128)(2,1)}), bf16[64,24,1024]{2,1,0:T(8,128)(2,1)}, u32[]{:S(2)}, u32[]{:S(2)}) async-start(bf16[64,24,1024]{2,1,0:T(8,128)(2,1)} %bitcast.66), calls=%async_computation.3 | async-start | bytes 6291456 | tf_op jit(solution)/shard_map/all_to_all | solution.py:104
  286.9 72.8 %all-to-all-done.3 = bf16[64,24,1024]{2,1,0:T(8,128)(2,1)} async-done(((bf16[64,24,1024]{2,1,0:T(8,128)(2,1)}), bf16[64,24,1024]{2,1,0:T(8,128)(2,1)}, u32[]{:S(2)}, u32[]{:S(2)}) %all-to-all-start.3) | async-done | bytes 3145760 | tf_op jit(solution)/shard_map/all_to_all | solution.py:104
  359.7 4.0 fusion.5
  363.7 4.8 %select_reduce_fusion = f32[1536,8]{1,0:T(8,128)S(1)} fusion(f32[1536,128]{1,0:T(8,128)S(1)} %fusion.5, s32[1536,8]{1,0:T(8,128)S(1)} %copy.57), kind=kLoop, calls=%fused_computation | loop fusion | flops 4706304 | bytes 884736 | tf_op jit(solution)/shard_map/reduce_sum | solution.py:25
  368.5 37.6 %all-reduce = (f32[1536,8]{1,0:T(8,128)S(1)}, f32[192]{0:T(256)S(1)}) all-reduce(f32[1536,8]{1,0:T(8,128)S(1)} %select_reduce_fusion, f32[192]{0:T(256)S(1)} %get-tuple-element.34), channel_id=1, replica_groups=mesh['lat'=64,'row'=8] {'row'}, use_global_device_ids=true, to_apply=%region_11.12 | all-reduce | flops 12480 | bytes 99840 | tf_op jit(solution)/shard_map/psum | solution.py:118
  406.1 3.1 slice_reduce_fusion.7
  409.3 3.8 select_convert_fusion
  413.0 0.8 convert_reduce_fusion
  413.9 4.7 %compare_select_fusion = (bf16[1536,2,128]{2,1,0:T(2,128)(2,1)S(1)}, bf16[1536,2,128]{2,1,0:T(2,128)(2,1)S(1)}) fusion(s32[2,128]{1,0:T(2,128)S(1)} %and_select_fusion.1, s32[1536]{0:T(1024)S(1)} %add_select_fusion, bf16[1536,128]{1,0:T(8,128)(2,1)S(1)} %select_convert_fusion.1, bf16[1536,128]{1,0:T(8,128)(2,1)S(1)} %select_convert_fusion), kind=kLoop, calls=%fused_computation.11 | loop fusion | flops 1179648 | bytes 2366464 | tf_op jit(solution)/shard_map/jit(_where)/select_n | solution.py:78
  419.2 3.7 convolution_convert_fusion.3
  422.9 3.7 convolution_convert_fusion.4
  (49 shorter events, 5.4 us)
Async XLA Ops:
  0.6 195.7 %copy-start = (bf16[256,1024]{1,0:T(8,128)(2,1)S(1)}, bf16[256,1024]{1,0:T(8,128)(2,1)}, u32[]{:S(2)}) copy-start(bf16[256,1024]{1,0:T(8,128)(2,1)} %param.11) | copy-start | bytes 1572868
  1.5 14.9 %copy-start.4 = (s32[192,4]{0,1:T(4,128)S(1)}, s32[192,4]{0,1:T(4,128)}, u32[]{:S(2)}) copy-start(s32[192,4]{0,1:T(4,128)} %param.12) | copy-start | bytes 9220
  2.6 14.8 %copy-start.1 = (f32[192,1024]{1,0:T(8,128)S(1)}, f32[192,1024]{1,0:T(8,128)}, u32[]{:S(2)}) copy-start(f32[192,1024]{1,0:T(8,128)} %param.7) | copy-start | bytes 2359300
  2.6 14.8 %copy-start.5 = (f32[1024]{0:T(1024)S(1)}, f32[1024]{0:T(1024)}, u32[]{:S(2)}) copy-start(f32[1024]{0:T(1024)} %param.8) | copy-start | bytes 12292
  5.6 19.7 %all-to-all-start.1 = ((s32[64,1,192]{2,1,0:T(1,128)}), s32[64,1,192]{2,1,0:T(1,128)S(1)}, u32[]{:S(2)}, u32[]{:S(2)}) async-start(s32[64,1,192]{2,1,0:T(1,128)} %reshape.843), calls=%async_computation.1 | async-start | bytes 131072 | tf_op jit(solution)/shard_map/all_to_all | solution.py:55
  25.3 6.5 %copy-start.3 = (bf16[1024,256]{1,0:T(8,128)(2,1)S(1)}, bf16[1024,256]{1,0:T(8,128)(2,1)}, u32[]{:S(2)}) copy-start(bf16[1024,256]{1,0:T(8,128)(2,1)} %param.9) | copy-start | bytes 1572868
  25.3 6.8 %copy-start.6 = (f32[256]{0:T(256)S(1)}, f32[256]{0:T(256)}, u32[]{:S(2)}) copy-start(f32[256]{0:T(256)} %param.10) | copy-start | bytes 3076
  25.3 79.4 %all-to-all-start = ((bf16[64,24,1024]{2,1,0:T(8,128)(2,1)}), bf16[64,24,1024]{2,1,0:T(8,128)(2,1)}, u32[]{:S(2)}, u32[]{:S(2)}) async-start(bf16[64,24,1024]{2,1,0:T(8,128)(2,1)} %bitcast.65), calls=%async_computation | async-start | bytes 6291456 | tf_op jit(solution)/shard_map/all_to_all | solution.py:58
  197.4 79.1 %copy-start.2 = (f32[192,1024]{1,0:T(8,128)S(1)}, f32[192,1024]{1,0:T(8,128)}, u32[]{:S(2)}) copy-start(f32[192,1024]{1,0:T(8,128)} %param.7) | copy-start | bytes 2359300
  280.2 79.5 %all-to-all-start.3 = ((bf16[64,24,1024]{2,1,0:T(8,128)(2,1)}), bf16[64,24,1024]{2,1,0:T(8,128)(2,1)}, u32[]{:S(2)}, u32[]{:S(2)}) async-start(bf16[64,24,1024]{2,1,0:T(8,128)(2,1)} %bitcast.66), calls=%async_computation.3 | async-start | bytes 6291456 | tf_op jit(solution)/shard_map/all_to_all | solution.py:104
